TPU v7x, 256 devices: a whole 4x4x8 slice. The times are simulated.
256 devices in a mesh: sample: 16 (over y, x_hi, core), filter: 16 (over x_lo, z).
Axes of the slice: x: 4 (x_hi: 2, x_lo: 2; x = x_hi * 2 + x_lo), y: 4, z: 8, core: 2. Of those that a mesh axis runs over, the one named last changes fastest.
Arguments:
- activations: bfloat16 [16, 2, 128, 2048], P('sample', None, None, 'filter'), may hold values from -18 to 18
- cotangent: bfloat16 [16, 2, 128, 2048], P('sample', None, None, 'filter'), may hold values from -2.5 to 2.5
- master_first: float32 [9, 2048, 2048], P(None, 'sample', 'filter'), may hold values from -0.046875 to 0.046875
- moment_first: float32 [9, 2048, 2048], P(None, 'sample', 'filter'), may hold values from -6 to 6
- second_first: float32 [9, 2048, 2048], P(None, 'sample', 'filter'), may hold values from 0.05 to 1
- master_second: float32 [9, 2048, 2048], P(None, 'sample', 'filter'), may hold values from -0.046875 to 0.046875
- moment_second: float32 [9, 2048, 2048], P(None, 'sample', 'filter'), may hold values from -6 to 6
- second_second: float32 [9, 2048, 2048], P(None, 'sample', 'filter'), may hold values from 0.05 to 1
Outputs:
- level_out: bfloat16 [16, 2, 128, 2048], P('sample', None, None, 'filter')
- input_grad: bfloat16 [16, 2, 128, 2048], P('sample', None, None, 'filter')
- new_master_first: float32 [9, 2048, 2048], P(None, 'sample', 'filter')
- new_moment_first: float32 [9, 2048, 2048], P(None, 'sample', 'filter')
- new_second_first: float32 [9, 2048, 2048], P(None, 'sample', 'filter')
- new_master_second: float32 [9, 2048, 2048], P(None, 'sample', 'filter')
- new_moment_second: float32 [9, 2048, 2048], P(None, 'sample', 'filter')
- new_second_second: float32 [9, 2048, 2048], P(None, 'sample', 'filter')
All inputs are finite; a program needn't handle non-finite values.
Results may differ from a plain program's by a relative error of at most 0.017.
Values may be sent and summed in bfloat16 or wider, within the bound.
No kernel may reach another device: no remote copies, remote signals or barrier semaphores. Data moves between devices by JAX's collectives and lax.ppermute only.
A program may use at most 128 MiB of HBM per device.

v0:
```python
import jax
import jax.numpy as jnp
from jax import lax
from jax.sharding import PartitionSpec as P

GROUP = 64
NORM_EPS = 1e-05
LEARN_RATE = 0.001
BETA_ONE = 0.9
BETA_TWO = 0.999
ADAM_EPS = 1e-08
CORRECT_ONE = 1.0 - 0.9**10
CORRECT_TWO = 1.0 - 0.999**10


def pad_slab(field):
    return jnp.pad(field, ((0, 0), (1, 1), (1, 1), (0, 0)))


def window(padded, row_start, column_start, height, breadth):
    return padded[:, row_start : row_start + height, column_start : column_start + breadth, :]


def conv_forward(source, weight):
    samples, height, breadth, depth_in = source.shape
    padded = pad_slab(source)
    summed = jnp.zeros((samples * height * breadth, weight.shape[2]), jnp.float32)
    for kernel_tap in range(9):
        shifted = window(padded, kernel_tap // 3, kernel_tap % 3, height, breadth)
        summed = summed + jnp.dot(
            shifted.reshape(samples * height * breadth, depth_in),
            weight[kernel_tap],
            preferred_element_type=jnp.float32,
        )
    return summed.reshape(samples, height, breadth, weight.shape[2])


def group_silu(pre_act):
    samples, height, breadth, depth_all = pre_act.shape
    grouped = pre_act.reshape(samples, height, breadth, depth_all // GROUP, GROUP)
    center = jnp.mean(grouped, axis=(1, 2, 4), keepdims=True)
    deviation = grouped - center
    spread = jnp.mean(deviation * deviation, axis=(1, 2, 4), keepdims=True)
    return jax.nn.silu(deviation * lax.rsqrt(spread + NORM_EPS)).reshape(pre_act.shape)


def tap_grads(source, upstream):
    samples, height, breadth, depth_in = source.shape
    padded = pad_slab(source)
    flat_up = upstream.reshape(samples, height * breadth, upstream.shape[3])
    results = []
    for kernel_tap in range(9):
        shifted = window(padded, kernel_tap // 3, kernel_tap % 3, height, breadth).reshape(
            samples, height * breadth, depth_in
        )
        results.append(
            lax.dot_general(
                shifted, flat_up, (((1,), (1,)), ((0,), (0,))), preferred_element_type=jnp.float32
            ).astype(jnp.bfloat16)
        )
    return jnp.stack(results, axis=1)


def adam_update(master, moment, second, gradient):
    moment_new = BETA_ONE * moment + (1.0 - BETA_ONE) * gradient
    second_new = BETA_TWO * second + (1.0 - BETA_TWO) * gradient * gradient
    step_size = moment_new / CORRECT_ONE / (jnp.sqrt(second_new / CORRECT_TWO) + ADAM_EPS)
    return (master - LEARN_RATE * step_size, moment_new, second_new)


def full_weight(master):
    return lax.all_gather(master.astype(jnp.bfloat16), "sample", axis=1, tiled=True)


def keep_panels(source):
    return lax.all_gather(source, "filter", axis=3, tiled=True)


def data_grad(upstream, weight):
    samples, height, breadth, depth_out = upstream.shape
    cell_count = samples * height * breadth
    padded = pad_slab(upstream)
    shifted_all = [
        window(padded, 2 - kernel_tap // 3, 2 - kernel_tap % 3, height, breadth).reshape(
            cell_count, depth_out
        )
        for kernel_tap in range(9)
    ]
    local_rows = weight.shape[1] // lax.axis_size("filter")
    summed = jnp.zeros((local_rows * lax.axis_size("filter"), cell_count), jnp.float32)
    for kernel_tap in range(9):
        summed = summed + lax.dot_general(
            weight[kernel_tap],
            shifted_all[kernel_tap],
            (((1,), (1,)), ((), ())),
            preferred_element_type=jnp.float32,
        )
    own_rows = lax.psum_scatter(
        summed.astype(jnp.bfloat16), "filter", scatter_dimension=0, tiled=True
    ).astype(jnp.float32)
    return own_rows.T.reshape(samples, height, breadth, local_rows)


def filter_grad(whole, upstream):
    partial_sum = tap_grads(whole, upstream)[0].astype(jnp.float32)
    return lax.psum_scatter(
        partial_sum.astype(jnp.bfloat16), "sample", scatter_dimension=1, tiled=True
    ).astype(jnp.float32)


def per_device(
    activations,
    cotangent,
    master_first,
    moment_first,
    second_first,
    master_second,
    moment_second,
    second_second,
):
    weight_first = full_weight(master_first)
    weight_second = full_weight(master_second)
    whole_input = keep_panels(activations)
    pre_first = conv_forward(whole_input, weight_first)
    hidden = group_silu(pre_first).astype(jnp.bfloat16)
    whole_hidden = keep_panels(hidden)
    pre_second = conv_forward(whole_hidden, weight_second)
    level_out = (activations.astype(jnp.float32) + pre_second).astype(jnp.bfloat16)
    hidden_grad = data_grad(cotangent, weight_second)
    _, pullback = jax.vjp(group_silu, pre_first)
    pre_grad = pullback(hidden_grad)[0].astype(jnp.bfloat16)
    input_grad = (cotangent.astype(jnp.float32) + data_grad(pre_grad, weight_first)).astype(
        jnp.bfloat16
    )
    grad_second = filter_grad(whole_hidden, cotangent)
    grad_first = filter_grad(whole_input, pre_grad)
    new_master_first, new_moment_first, new_second_first = adam_update(
        master_first, moment_first, second_first, grad_first
    )
    new_master_second, new_moment_second, new_second_second = adam_update(
        master_second, moment_second, second_second, grad_second
    )
    return (
        level_out,
        input_grad,
        new_master_first,
        new_moment_first,
        new_second_first,
        new_master_second,
        new_moment_second,
        new_second_second,
    )


def solution(mesh):
    placed = (
        P("sample", None, None, "filter"),
        P("sample", None, None, "filter"),
        P(None, "sample", "filter"),
        P(None, "sample", "filter"),
        P(None, "sample", "filter"),
        P(None, "sample", "filter"),
        P(None, "sample", "filter"),
        P(None, "sample", "filter"),
    )
    return jax.shard_map(
        per_device,
        mesh=mesh,
        in_specs=placed,
        out_specs=(
            P("sample", None, None, "filter"),
            P("sample", None, None, "filter"),
            P(None, "sample", "filter"),
            P(None, "sample", "filter"),
            P(None, "sample", "filter"),
            P(None, "sample", "filter"),
            P(None, "sample", "filter"),
            P(None, "sample", "filter"),
        ),
        check_vma=False,
    )
```

profile of v0, /device:TPU:32, one launch (start us, length us, event | category | flops | bytes accessed | tf_op | source)
XLA Modules:
  0.0 662.6 jit_solution(3601517996749550026)
XLA Ops:
  7.9 1.8 convert_element_type.155
  9.8 66.3 %all-gather.5.cloned.1.call-done = bf16[1,2,128,2048]{3,2,1,0:T(8,128)(2,1)} async-done(((bf16[1,2,128,128]{3,2,1,0:T(8,128)(2,1)}), bf16[1,2,128,2048]{3,2,1,0:T(8,128)(2,1)}) %all-gather.5.cloned.1.call-update) | async-done | bytes 1048592 | tf_op jit(solution)/shard_map/all_gather | solution.py:76
  76.1 5.0 pad_slice_fusion.8
  81.1 60.8 %all-gather.7.cloned.1.call-done = bf16[9,2048,128]{2,1,0:T(8,128)(2,1)} async-done(((bf16[9,128,128]{2,1,0:T(8,128)(2,1)}), bf16[9,2048,128]{2,1,0:T(8,128)(2,1)}) %all-gather.7.cloned.1.call-update) | async-done | bytes 4718608 | tf_op jit(solution)/shard_map/all_gather | solution.py:72
  141.9 1.9 fusion.67
  143.9 2.3 convolution_add_fusion.27
  146.2 1.8 convolution_add_fusion.26
  148.0 1.7 convolution_add_fusion.25
  153.6 66.1 %all-gather.9.cloned.1.call-done = bf16[1,2,128,2048]{2,3,1,0:T(8,128)(2,1)} async-done(((bf16[1,2,128,128]{2,3,1,0:T(8,128)(2,1)}), bf16[1,2,128,2048]{2,3,1,0:T(8,128)(2,1)}) %all-gather.9.cloned.1.call-update) | async-done | bytes 1048592 | tf_op jit(solution)/shard_map/all_gather | solution.py:76
  219.8 1.6 fusion.52
  221.4 1.6 fusion.50
  223.0 1.6 fusion.48
  228.2 2.1 copy-done.9
  230.4 88.9 %reduce-scatter.11.cloned.1.call-done = bf16[9,128,128]{2,1,0:T(8,128)(2,1)} async-done(((bf16[9,2048,128]{2,1,0:T(8,128)(2,1)}), bf16[9,128,128]{2,1,0:T(8,128)(2,1)}) %reduce-scatter.11.cloned.1.call-update) | async-done | bytes 294928 | tf_op jit(solution)/shard_map/reduce_scatter | solution.py:106
  319.3 3.3 multiply_subtract_fusion
  323.7 59.9 %all-gather.11.cloned.1.call-done = bf16[9,2048,128]{2,1,0:T(8,128)(2,1)} async-done(((bf16[9,128,128]{2,1,0:T(8,128)(2,1)}), bf16[9,2048,128]{2,1,0:T(8,128)(2,1)}) %all-gather.11.cloned.1.call-update) | async-done | bytes 4718608 | tf_op jit(solution)/shard_map/all_gather | solution.py:72
  383.6 1.7 fusion.68
  385.3 1.5 convolution_bitcast_fusion.1
  389.5 1.6 fusion.6
  391.1 2.3 copy.67
  393.5 68.0 %reduce-scatter.13.cloned.1.call-done = bf16[128,256]{1,0:T(8,128)(2,1)} async-done(((bf16[2048,256]{1,0:T(8,128)(2,1)}), bf16[128,256]{1,0:T(8,128)(2,1)}) %reduce-scatter.13.cloned.1.call-update) | async-done | bytes 65552
  461.5 0.9 copy.68
  466.3 2.5 fusion.18
  468.8 1.7 copy.54
  470.5 1.1 fusion.76
  472.3 1.6 copy.56
  473.9 1.6 copy.57
  475.5 1.6 copy.58
  478.0 1.0 copy.62
  479.0 1.0 copy.63
  480.0 1.7 fusion.66
  481.7 1.6 convolution_add_fusion.7
  483.3 1.5 convolution_add_fusion.6
  487.0 1.4 fusion.7
  488.5 2.3 copy.69
  491.0 2.7 fusion.20
  493.7 2.5 fusion.22
  496.3 2.5 fusion.24
  498.8 1.3 fusion.26
  500.1 1.3 fusion.28
  501.4 1.3 fusion.30
  502.8 1.3 fusion.32
  504.1 1.3 fusion.34
  505.4 3.6 pad_slice_fusion
  509.0 2.3 copy.44
  511.3 2.3 copy.45
  513.5 2.3 copy.46
  515.8 2.3 copy.47
  518.1 2.3 copy.49
  520.4 2.3 copy.50
  522.7 1.4 copy.51
  524.6 1.3 copy.48
  525.9 1.9 fusion.69
  527.8 1.9 convolution_add_fusion.19
  529.7 1.9 convolution_add_fusion.18
  531.6 1.5 convolution_add_fusion.17
  533.1 1.5 convolution_add_fusion.16
  534.6 1.5 convolution_add_fusion.15
  536.1 1.5 convolution_add_fusion.14
  537.6 1.5 convolution_add_fusion.13
  539.1 1.5 convolution_add_fusion.12
  540.5 18.8 %reduce-scatter.15.cloned.1.call-done = bf16[128,256]{1,0:T(8,128)(2,1)} async-done(((bf16[2048,256]{1,0:T(8,128)(2,1)}), bf16[128,256]{1,0:T(8,128)(2,1)}) %reduce-scatter.15.cloned.1.call-update) | async-done | bytes 65552
  561.0 91.8 %reduce-scatter.9.cloned.1.call-done = bf16[9,128,128]{2,1,0:T(8,128)(2,1)} async-done(((bf16[9,2048,128]{2,1,0:T(8,128)(2,1)}), bf16[9,128,128]{2,1,0:T(8,128)(2,1)}) %reduce-scatter.9.cloned.1.call-update) | async-done | bytes 294928 | tf_op jit(solution)/shard_map/reduce_scatter | solution.py:106
  652.7 3.0 multiply_subtract_fusion.1
  (128 shorter events, 22.4 us)
Async XLA Ops:
  7.2 69.0 %all-gather.5.cloned.1.call-start = ((), (), s32[]{:S(2)}) async-start(), calls=%async_computation.4 | async-start | bytes 1114112 | tf_op jit(solution)/shard_map/all_gather | solution.py:76
  7.9 134.0 %all-gather.7.cloned.1.call-start = ((), (), s32[]{:S(2)}) async-start(), calls=%async_computation.5 | async-start | bytes 5013504 | tf_op jit(solution)/shard_map/all_gather | solution.py:72
  9.8 209.9 %all-gather.9.cloned.1.call-start = ((), (), s32[]{:S(2)}) async-start(), calls=%async_computation.6 | async-start | bytes 1114112 | tf_op jit(solution)/shard_map/all_gather | solution.py:76
  141.9 6.1 copy-start.1
  141.9 7.8 %copy-start.2 = (bf16[1,2,128,2048]{3,2,1,0:T(8,128)(2,1)S(1)}, bf16[1,2,128,2048]{3,2,1,0:T(8,128)(2,1)}, u32[]{:S(2)}) copy-start(bf16[1,2,128,2048]{3,2,1,0:T(8,128)(2,1)} %all-gather.5.cloned.1.call-done) | copy-start | bytes 3145732
  141.9 8.2 %copy-start.5 = (bf16[1,2,128,2048]{3,2,1,0:T(8,128)(2,1)S(1)}, bf16[1,2,128,2048]{3,2,1,0:T(8,128)(2,1)}, u32[]{:S(2)}) copy-start(bf16[1,2,128,2048]{3,2,1,0:T(8,128)(2,1)} %get-tuple-element.28) | copy-start | bytes 3145732
  143.9 6.7 %copy-start.3 = (bf16[1,2,128,2048]{3,2,1,0:T(8,128)(2,1)S(1)}, bf16[1,2,128,2048]{3,2,1,0:T(8,128)(2,1)}, u32[]{:S(2)}) copy-start(bf16[1,2,128,2048]{3,2,1,0:T(8,128)(2,1)} %get-tuple-element.29) | copy-start | bytes 3145732
  149.7 70.1 %copy-start.15 = (bf16[1,2,128,128]{3,2,1,0:T(8,128)(2,1)S(1)}, bf16[1,2,128,128]{3,2,1,0:T(8,128)(2,1)}, u32[]{:S(2)}) copy-start(bf16[1,2,128,128]{3,2,1,0:T(8,128)(2,1)} %param.9) | copy-start | bytes 196612
  152.5 73.3 %copy-start.24 = (f32[2]{0:T(128)}, f32[2]{0:T(128)S(1)}, u32[]{:S(2)}) copy-start(f32[2]{0:T(128)S(1)} %reduce_sum.85) | copy-start | bytes 28
  153.6 165.8 %reduce-scatter.11.cloned.1.call-start = ((), (), s32[]{:S(2)}) async-start(), calls=%async_computation.9 | async-start | bytes 5013504 | tf_op jit(solution)/shard_map/reduce_scatter | solution.py:106
  219.8 4.8 copy-start.7
  228.2 2.1 copy-start.9
  230.4 153.2 %all-gather.11.cloned.1.call-start = ((), (), s32[]{:S(2)}) async-start(), calls=%async_computation.7 | async-start | bytes 5013504 | tf_op jit(solution)/shard_map/all_gather | solution.py:72
  322.6 138.9 %reduce-scatter.13.cloned.1.call-start = ((), (), s32[]{:S(2)}) async-start(), calls=%async_computation.10 | async-start | bytes 1114112
  383.6 3.2 copy-start
  383.6 3.2 copy-start.23
  383.6 3.6 copy-start.22
  383.6 4.1 copy-start.18
  386.8 1.4 copy-start.17
  387.7 0.9 copy-start.16
  393.4 165.9 %reduce-scatter.15.cloned.1.call-start = ((), (), s32[]{:S(2)}) async-start(), calls=%async_computation.11 | async-start | bytes 1114112
  480.0 3.3 copy-start.20
  480.0 4.8 slice-start
  481.7 3.1 slice-start.1
  481.7 3.1 copy-start.19
  490.8 162.0 %reduce-scatter.9.cloned.1.call-start = ((), (), s32[]{:S(2)}) async-start(), calls=%async_computation.8 | async-start | bytes 5013504 | tf_op jit(solution)/shard_map/reduce_scatter | solution.py:106
  491.0 9.1 %copy-start.6 = (bf16[1,2,128,2048]{3,2,1,0:T(8,128)(2,1)S(1)}, bf16[1,2,128,2048]{3,2,1,0:T(8,128)(2,1)}, u32[]{:S(2)}) copy-start(bf16[1,2,128,2048]{3,2,1,0:T(8,128)(2,1)} %get-tuple-element.28) | copy-start | bytes 3145732
  491.0 10.4 %copy-start.4 = (bf16[1,2,128,2048]{3,2,1,0:T(8,128)(2,1)S(1)}, bf16[1,2,128,2048]{3,2,1,0:T(8,128)(2,1)}, u32[]{:S(2)}) copy-start(bf16[1,2,128,2048]{3,2,1,0:T(8,128)(2,1)} %get-tuple-element.29) | copy-start | bytes 3145732
  501.4 3.9 copy-start.8
  525.9 5.7 copy-start.13
  525.9 7.2 %copy-start.14 = (bf16[1,2,128,2048]{3,2,1,0:T(8,128)(2,1)S(1)}, bf16[1,2,128,2048]{3,2,1,0:T(8,128)(2,1)}, u32[]{:S(2)}) copy-start(bf16[1,2,128,2048]{3,2,1,0:T(8,128)(2,1)} %copy.48) | copy-start | bytes 3145732
  525.9 8.7 %copy-start.12 = (bf16[1,2,128,2048]{3,2,1,0:T(8,128)(2,1)S(1)}, bf16[1,2,128,2048]{3,2,1,0:T(8,128)(2,1)}, u32[]{:S(2)}) copy-start(bf16[1,2,128,2048]{3,2,1,0:T(8,128)(2,1)} %copy.49) | copy-start | bytes 3145732
  527.8 8.3 %copy-start.11 = (bf16[1,2,128,2048]{3,2,1,0:T(8,128)(2,1)S(1)}, bf16[1,2,128,2048]{3,2,1,0:T(8,128)(2,1)}, u32[]{:S(2)}) copy-start(bf16[1,2,128,2048]{3,2,1,0:T(8,128)(2,1)} %copy.50) | copy-start | bytes 3145732
  529.7 7.9 %copy-start.10 = (bf16[1,2,128,2048]{3,2,1,0:T(8,128)(2,1)S(1)}, bf16[1,2,128,2048]{3,2,1,0:T(8,128)(2,1)}, u32[]{:S(2)}) copy-start(bf16[1,2,128,2048]{3,2,1,0:T(8,128)(2,1)} %copy.51) | copy-start | bytes 3145732
  533.1 27.2 %copy-start.21 = (bf16[1,2,128,128]{3,2,1,0:T(8,128)(2,1)S(1)}, bf16[1,2,128,128]{3,2,1,0:T(8,128)(2,1)}, u32[]{:S(2)}) copy-start(bf16[1,2,128,128]{3,2,1,0:T(8,128)(2,1)} %param.8) | copy-start | bytes 196612
Sparse Core Ops, SparseCore 0:
  9.7 66.3 all-gather.4
  79.4 62.4 all-gather.6
  153.7 65.9 all-gather.8
  230.5 88.8 reduce-scatter.10
  322.7 60.7 all-gather.10
  393.6 67.8 reduce-scatter.12
  490.9 68.3 reduce-scatter.14
  563.7 88.9 reduce-scatter.8
where the time goes:
time: 664 us; the launch traced here: 663 us
  waiting for transfers between devices  521 us (78%)
  matrix products  65.3 us (10%)
  local copies, waits for them, and re-layouts  46.1 us (7%)
  between operations  14.8 us (2%)
  other arithmetic  14.2 us (2%)
    reduce_scatter x2, waiting for transfers between devices, filter_grad(): lax.psum_scatter(partial_sum.astype(jnp.bfloat16), 'sample', scatter_dime...  181 us
    all_gather x2, waiting for transfers between devices, keep_panels(): return lax.all_gather(source, 'filter', axis=3, tiled=True)  132 us
    all_gather x2, waiting for transfers between devices, full_weight(): lax.all_gather(master.astype(jnp.bfloat16), 'sample', axis=1, tiled=True)  121 us
    unnamed x10, waiting for transfers between devices  87.6 us
    slice x20, local copies, waits for them, and re-layouts, window(): padded[:, row_start:row_start + height, column_start:column_start + bread...  33.4 us
    dot_general x18, matrix products, tap_grads(): lax.dot_general(shifted, flat_up, (((1,), (1,)), ((0,), (0,))), preferred...  25.2 us
    dot_general x18, matrix products, conv_forward(): jnp.dot(shifted.reshape(samples * height * breadth, depth_in), weight[ker...  24.4 us
    dot_general x18, matrix products, data_grad(): lax.dot_general(weight[kernel_tap], shifted_all[kernel_tap], (((1,), (1,)...  15.7 us
  transfers between devices with their start and end apart: 8, of which 8 were waited for; matrix products, arithmetic and copies ran while one was open for 9% of the time, Pallas kernels for 0%

commit v1 on v0

--- a/solution.py
+++ b/solution.py
@@ -73,7 +73,9 @@
 
 
 def keep_panels(source):
-    return lax.all_gather(source, "filter", axis=3, tiled=True)
+    return jnp.concatenate(
+        lax.all_to_all(jnp.stack([source] * lax.axis_size("filter")), "filter", 0, 0), axis=3
+    )
 
 
 def data_grad(upstream, weight):

time: 664 us -> 562 us (0.85)
  waiting for transfers between devices: 521 us -> 341 us
  blocking collectives: 0 us -> 69.8 us
    all_gather x2 -> x0, waiting for transfers between devices: 132 us -> none  [keep_panels(): return lax.all_gather(source, 'filter', axis=3, tiled=True)]
    all_to_all x0 -> x2, blocking collectives: none -> 69.8 us  [keep_panels(): lax.all_to_all(jnp.stack([source] * lax.axis_size('filter')), 'filter', 0...]
    all_gather x2, waiting for transfers between devices: 121 us -> 73.8 us  [full_weight(): lax.all_gather(master.astype(jnp.bfloat16), 'sample', axis=1, tiled=True)]
    unnamed x10 -> x8, waiting for transfers between devices: 87.6 us -> 89.4 us
  transfers between devices with their start and end apart: 8 -> 6, of which waited for: 8 -> 6; matrix products, arithmetic and copies ran while one was open for 9% -> 12% of each run, Pallas kernels for 0% -> 0%
where the time goes in v1:
time: 562 us; the launch traced here: 561 us
  waiting for transfers between devices  341 us (61%)
  matrix products  71.3 us (13%)
  blocking collectives  69.8 us (12%)
  local copies, waits for them, and re-layouts  51.5 us (9%)
  between operations  14.7 us (3%)
  other arithmetic  11.8 us (2%)
    reduce_scatter x2, waiting for transfers between devices, filter_grad(): lax.psum_scatter(partial_sum.astype(jnp.bfloat16), 'sample', scatter_dime...  178 us
    unnamed x8, waiting for transfers between devices  89.4 us
    all_gather x2, waiting for transfers between devices, full_weight(): lax.all_gather(master.astype(jnp.bfloat16), 'sample', axis=1, tiled=True)  73.8 us
    all_to_all x2, blocking collectives, keep_panels(): lax.all_to_all(jnp.stack([source] * lax.axis_size('filter')), 'filter', 0...  69.8 us
    slice x20, local copies, waits for them, and re-layouts, window(): padded[:, row_start:row_start + height, column_start:column_start + bread...  35.8 us
    dot_general x18, matrix products, tap_grads(): lax.dot_general(shifted, flat_up, (((1,), (1,)), ((0,), (0,))), preferred...  31.8 us
    dot_general x18, matrix products, conv_forward(): jnp.dot(shifted.reshape(samples * height * breadth, depth_in), weight[ker...  23.9 us
    dot_general x18, matrix products, data_grad(): lax.dot_general(weight[kernel_tap], shifted_all[kernel_tap], (((1,), (1,)...  15.6 us
  transfers between devices with their start and end apart: 6, of which 6 were waited for; matrix products, arithmetic and copies ran while one was open for 12% of the time, Pallas kernels for 0%

profile of v1, /device:TPU:32, one launch (start us, length us, event | category | flops | bytes accessed | tf_op | source)
XLA Modules:
  0.0 561.0 jit_solution(617416613159496535)
XLA Ops:
  7.2 1.8 convert_element_type.154
  10.3 35.5 %all_to_all.10 = bf16[16,1,2,128,128]{3,4,2,1,0:T(8,128)(2,1)S(1)} all-to-all(bf16[16,1,2,128,128]{3,4,2,1,0:T(8,128)(2,1)S(1)} %stack.44), channel_id=1, replica_groups=mesh['sample'=16,'filter'=16] {'filter'}, dimensions={0} | all-to-all | bytes 2097152 | tf_op jit(solution)/shard_map/all_to_all | solution.py:77
  45.9 1.7 copy.59
  47.6 3.7 pad_slice_fusion.8
  51.3 2.4 copy.63
  53.7 2.3 copy.56
  56.0 2.3 copy.57
  58.3 1.3 copy.58
  60.6 1.5 copy.62
  62.1 2.3 copy.55
  64.4 13.7 %all-gather.3.cloned.1.call-done = bf16[9,2048,128]{2,1,0:T(8,128)(2,1)} async-done(((bf16[9,128,128]{2,1,0:T(8,128)(2,1)}), bf16[9,2048,128]{2,1,0:T(8,128)(2,1)}) %all-gather.3.cloned.1.call-update) | async-done | bytes 4718608 | tf_op jit(solution)/shard_map/all_gather | solution.py:72
  78.1 1.9 fusion.73
  80.1 2.0 convolution_add_fusion.27
  82.1 1.8 convolution_add_fusion.26
  83.9 1.7 convolution_add_fusion.25
  89.0 34.3 %all_to_all.11 = bf16[16,1,2,128,128]{4,3,2,1,0:T(8,128)(2,1)S(1)} all-to-all(bf16[16,1,2,128,128]{4,3,2,1,0:T(8,128)(2,1)S(1)} %stack.45), channel_id=1, replica_groups=mesh['sample'=16,'filter'=16] {'filter'}, dimensions={0} | all-to-all | bytes 2097152 | tf_op jit(solution)/shard_map/all_to_all | solution.py:77
  124.2 1.6 copy.69
  125.9 2.3 copy.64
  128.2 2.5 fusion.51
  130.7 2.3 fusion.49
  132.9 2.3 fusion.47
  135.3 1.4 fusion.45
  136.7 1.3 fusion.35
  138.0 1.4 fusion.43
  143.2 86.4 %reduce-scatter.11.cloned.1.call-done = bf16[9,128,128]{2,1,0:T(8,128)(2,1)} async-done(((bf16[9,2048,128]{2,1,0:T(8,128)(2,1)}), bf16[9,128,128]{2,1,0:T(8,128)(2,1)}) %reduce-scatter.11.cloned.1.call-update) | async-done | bytes 294928 | tf_op jit(solution)/shard_map/reduce_scatter | solution.py:108
  229.7 3.3 multiply_subtract_fusion
  233.7 60.1 %all-gather.5.cloned.1.call-done = bf16[9,2048,128]{2,1,0:T(8,128)(2,1)} async-done(((bf16[9,128,128]{2,1,0:T(8,128)(2,1)}), bf16[9,2048,128]{2,1,0:T(8,128)(2,1)}) %all-gather.5.cloned.1.call-update) | async-done | bytes 4718608 | tf_op jit(solution)/shard_map/all_gather | solution.py:72
  293.9 1.7 convolution_bitcast_fusion
  295.5 1.5 convolution_bitcast_fusion.1
  299.8 1.6 fusion.6
  301.3 2.3 copy.78
  303.7 68.1 %reduce-scatter.13.cloned.1.call-done = bf16[128,256]{1,0:T(8,128)(2,1)} async-done(((bf16[2048,256]{1,0:T(8,128)(2,1)}), bf16[128,256]{1,0:T(8,128)(2,1)}) %reduce-scatter.13.cloned.1.call-update) | async-done | bytes 65552
  376.0 2.5 fusion.17
  378.6 1.6 fusion.72
  380.2 1.5 convolution_add_fusion.7
  381.7 1.5 convolution_add_fusion.6
  385.5 1.4 fusion.7
  386.9 2.3 copy.80
  389.5 2.6 fusion.19
  392.1 2.6 fusion.21
  394.7 2.5 fusion.23
  397.2 1.4 fusion.25
  399.9 1.3 fusion.29
  402.5 1.3 fusion.33
  403.9 3.6 pad_slice_fusion
  407.5 2.3 copy.73
  409.8 2.4 copy.66
  412.1 2.3 copy.67
  414.4 2.3 copy.68
  416.7 2.3 copy.70
  419.0 1.3 copy.71
  420.3 1.4 copy.72
  422.2 1.6 fusion.75
  423.8 1.9 convolution_add_fusion.19
  425.7 1.6 convolution_add_fusion.18
  427.3 1.9 convolution_add_fusion.17
  429.2 1.5 convolution_add_fusion.16
  430.7 1.5 convolution_add_fusion.15
  432.2 1.5 convolution_add_fusion.14
  433.7 1.5 convolution_add_fusion.13
  435.1 1.5 convolution_add_fusion.12
  436.6 21.2 %reduce-scatter.15.cloned.1.call-done = bf16[128,256]{1,0:T(8,128)(2,1)} async-done(((bf16[2048,256]{1,0:T(8,128)(2,1)}), bf16[128,256]{1,0:T(8,128)(2,1)}) %reduce-scatter.15.cloned.1.call-update) | async-done | bytes 65552
  459.5 91.7 %reduce-scatter.9.cloned.1.call-done = bf16[9,128,128]{2,1,0:T(8,128)(2,1)} async-done(((bf16[9,2048,128]{2,1,0:T(8,128)(2,1)}), bf16[9,128,128]{2,1,0:T(8,128)(2,1)}) %reduce-scatter.9.cloned.1.call-update) | async-done | bytes 294928 | tf_op jit(solution)/shard_map/reduce_scatter | solution.py:108
  551.2 3.0 multiply_subtract_fusion.1
  (126 shorter events, 25.6 us)
Async XLA Ops:
  7.2 71.0 %all-gather.3.cloned.1.call-start = ((), (), s32[]{:S(2)}) async-start(), calls=%async_computation.6 | async-start | bytes 5013504 | tf_op jit(solution)/shard_map/all_gather | solution.py:72
  9.1 220.6 %reduce-scatter.11.cloned.1.call-start = ((), (), s32[]{:S(2)}) async-start(), calls=%async_computation.9 | async-start | bytes 5013504 | tf_op jit(solution)/shard_map/reduce_scatter | solution.py:108
  51.3 6.9 %copy-start.8 = (bf16[1,2,128,2048]{2,3,1,0:T(8,128)(2,1)S(1)}, bf16[1,2,128,2048]{2,3,1,0:T(8,128)(2,1)}, u32[]{:S(2)}) copy-start(bf16[1,2,128,2048]{2,3,1,0:T(8,128)(2,1)} %get-tuple-element.27) | copy-start | bytes 3145732
  78.1 5.8 %copy-start.1 = (bf16[9,2048,128]{2,1,0:T(8,128)(2,1)S(1)}, bf16[9,2048,128]{2,1,0:T(8,128)(2,1)}, u32[]{:S(2)}) copy-start(bf16[9,2048,128]{2,1,0:T(8,128)(2,1)} %all-gather.3.cloned.1.call-done) | copy-start | bytes 14155780
  78.1 7.5 %copy-start.14 = (bf16[1,2,128,16,128]{4,3,2,1,0:T(8,128)(2,1)S(1)}, bf16[1,2,128,16,128]{4,3,2,1,0:T(8,128)(2,1)}, u32[]{:S(2)}) copy-start(bf16[1,2,128,16,128]{4,3,2,1,0:T(8,128)(2,1)} %copy.59) | copy-start | bytes 3145732
  83.9 3.5 copy-start.2
  87.4 40.8 %copy-start.18 = (bf16[1,2,128,128]{3,2,1,0:T(8,128)(2,1)S(1)}, bf16[1,2,128,128]{3,2,1,0:T(8,128)(2,1)}, u32[]{:S(2)}) copy-start(bf16[1,2,128,128]{3,2,1,0:T(8,128)(2,1)} %param.9) | copy-start | bytes 196612
  88.5 42.2 %copy-start.23 = (f32[2]{0:T(128)}, f32[2]{0:T(128)S(1)}, u32[]{:S(2)}) copy-start(f32[2]{0:T(128)S(1)} %reduce_sum.85) | copy-start | bytes 28
  123.3 1.0 copy-start.4
  128.2 7.1 %copy-start.5 = (bf16[1,2,128,16,128]{2,4,3,1,0:T(8,128)(2,1)S(1)}, bf16[1,2,128,16,128]{2,4,3,1,0:T(8,128)(2,1)}, u32[]{:S(2)}) copy-start(bf16[1,2,128,16,128]{2,4,3,1,0:T(8,128)(2,1)} %copy.64) | copy-start | bytes 3145732
  128.2 8.5 %copy-start.16 = (bf16[1,2,128,16,128]{4,3,2,1,0:T(8,128)(2,1)S(1)}, bf16[1,2,128,16,128]{4,3,2,1,0:T(8,128)(2,1)}, u32[]{:S(2)}) copy-start(bf16[1,2,128,16,128]{4,3,2,1,0:T(8,128)(2,1)} %copy.69) | copy-start | bytes 3145732
  143.2 150.7 %all-gather.5.cloned.1.call-start = ((), (), s32[]{:S(2)}) async-start(), calls=%async_computation.7 | async-start | bytes 5013504 | tf_op jit(solution)/shard_map/all_gather | solution.py:72
  232.9 138.8 %reduce-scatter.13.cloned.1.call-start = ((), (), s32[]{:S(2)}) async-start(), calls=%async_computation.10 | async-start | bytes 1114112
  293.9 3.2 copy-start
  293.9 3.2 copy-start.22
  293.9 3.6 copy-start.21
  293.9 4.1 copy-start.19
  303.6 154.2 %reduce-scatter.15.cloned.1.call-start = ((), (), s32[]{:S(2)}) async-start(), calls=%async_computation.11 | async-start | bytes 1114112
  378.6 4.7 slice-start
  380.2 3.1 slice-start.1
  389.2 162.0 %reduce-scatter.9.cloned.1.call-start = ((), (), s32[]{:S(2)}) async-start(), calls=%async_computation.8 | async-start | bytes 5013504 | tf_op jit(solution)/shard_map/reduce_scatter | solution.py:108
  389.5 7.7 %copy-start.15 = (bf16[1,2,128,16,128]{4,3,2,1,0:T(8,128)(2,1)S(1)}, bf16[1,2,128,16,128]{4,3,2,1,0:T(8,128)(2,1)}, u32[]{:S(2)}) copy-start(bf16[1,2,128,16,128]{4,3,2,1,0:T(8,128)(2,1)} %copy.59) | copy-start | bytes 3145732
  392.1 10.4 %copy-start.3 = (bf16[1,2,128,2048]{3,2,1,0:T(8,128)(2,1)S(1)}, bf16[1,2,128,2048]{3,2,1,0:T(8,128)(2,1)}, u32[]{:S(2)}) copy-start(bf16[1,2,128,2048]{3,2,1,0:T(8,128)(2,1)} %copy.63) | copy-start | bytes 3145732
  399.9 4.0 copy-start.6
  409.8 9.2 %copy-start.7 = (bf16[1,2,128,2048]{2,3,1,0:T(8,128)(2,1)S(1)}, bf16[1,2,128,2048]{2,3,1,0:T(8,128)(2,1)}, u32[]{:S(2)}) copy-start(bf16[1,2,128,2048]{2,3,1,0:T(8,128)(2,1)} %get-tuple-element.21) | copy-start | bytes 3145732
  420.3 5.4 copy-start.13
  422.1 7.0 %copy-start.17 = (bf16[1,2,128,16,128]{4,3,2,1,0:T(8,128)(2,1)S(1)}, bf16[1,2,128,16,128]{4,3,2,1,0:T(8,128)(2,1)}, u32[]{:S(2)}) copy-start(bf16[1,2,128,16,128]{4,3,2,1,0:T(8,128)(2,1)} %copy.69) | copy-start | bytes 3145732
  422.2 8.5 %copy-start.12 = (bf16[1,2,128,2048]{3,2,1,0:T(8,128)(2,1)S(1)}, bf16[1,2,128,2048]{3,2,1,0:T(8,128)(2,1)}, u32[]{:S(2)}) copy-start(bf16[1,2,128,2048]{3,2,1,0:T(8,128)(2,1)} %copy.70) | copy-start | bytes 3145732
  423.8 8.4 %copy-start.11 = (bf16[1,2,128,2048]{3,2,1,0:T(8,128)(2,1)S(1)}, bf16[1,2,128,2048]{3,2,1,0:T(8,128)(2,1)}, u32[]{:S(2)}) copy-start(bf16[1,2,128,2048]{3,2,1,0:T(8,128)(2,1)} %copy.71) | copy-start | bytes 3145732
  425.7 8.0 %copy-start.10 = (bf16[1,2,128,2048]{3,2,1,0:T(8,128)(2,1)S(1)}, bf16[1,2,128,2048]{3,2,1,0:T(8,128)(2,1)}, u32[]{:S(2)}) copy-start(bf16[1,2,128,2048]{3,2,1,0:T(8,128)(2,1)} %copy.72) | copy-start | bytes 3145732
  427.3 7.9 %copy-start.9 = (bf16[1,2,128,2048]{3,2,1,0:T(8,128)(2,1)S(1)}, bf16[1,2,128,2048]{3,2,1,0:T(8,128)(2,1)}, u32[]{:S(2)}) copy-start(bf16[1,2,128,2048]{3,2,1,0:T(8,128)(2,1)} %copy.73) | copy-start | bytes 3145732
  429.2 29.7 %copy-start.20 = (bf16[1,2,128,128]{3,2,1,0:T(8,128)(2,1)S(1)}, bf16[1,2,128,128]{3,2,1,0:T(8,128)(2,1)}, u32[]{:S(2)}) copy-start(bf16[1,2,128,128]{3,2,1,0:T(8,128)(2,1)} %param.8) | copy-start | bytes 196612
Sparse Core Ops, SparseCore 0:
  11.3 66.7 all-gather.2
  143.3 86.3 reduce-scatter.10
  233.1 60.7 all-gather.4
  303.8 67.9 reduce-scatter.12
  389.4 68.4 reduce-scatter.14
  462.1 89.0 reduce-scatter.8
